TPU v7x, 256 devices: a whole 4x4x8 slice. The times are simulated.
256 devices in a mesh: dp: 4 (over x), seq: 4 (over y_hi, core), tensor: 16 (over y_lo, z).
Axes of the slice: x: 4, y: 4 (y_hi: 2, y_lo: 2; y = y_hi * 2 + y_lo), z: 8, core: 2. Of those that a mesh axis runs over, the one named last changes fastest.
Arguments:
- byte_acts: bfloat16 [4, 16384, 2048], P('dp', 'seq', 'tensor'), may hold values from -18 to 18
- conv_weight: bfloat16 [16, 1024, 128], P('tensor'), may hold values from -0.1875 to 0.1875
- conv_bias: float32 [2048], P('tensor'), may hold values from -3 to 3
- proj_weight: bfloat16 [2048, 8192], P(None, 'tensor'), may hold values from -0.125 to 0.125
- teacher: bfloat16 [4, 4096, 8192], P('dp', 'seq', 'tensor'), may hold values from -6 to 6
- span_lengths: int32 [4, 4096], P('dp'), may hold values from 1 to 16, as said below
Outputs:
- downsampled: bfloat16 [4, 4096, 2048], P('dp', 'seq', 'tensor')
- byte_grad: bfloat16 [4, 16384, 2048], P('dp', 'seq', 'tensor')
- conv_grad: float32 [16, 1024, 128], P('tensor')
- proj_grad: float32 [2048, 8192], P(None, 'tensor')
Inputs may be any that keep to these rules, and one draw needn't show every extreme that they name: `span_lengths`: each document's 4096 span lengths cover its 16384 bytes in order; the longest is exactly 16.
All inputs are finite; a program needn't handle non-finite values.
Results may differ from a plain program's by a relative error of at most 0.019.
Values may be sent and summed in bfloat16 or wider, within the bound.
No kernel may reach another device: no remote copies, remote signals or barrier semaphores. Data moves between devices by JAX's collectives and lax.ppermute only.
A program may use at most 64 MiB of HBM per device.

v0:
```python
import jax
import jax.numpy as jnp
from jax import lax
from jax.sharding import PartitionSpec as P

STRIDE = 4
KERNEL = 8


def shifted(block, axis, distance):
    devices = range(lax.axis_size(axis))
    route = [(i - distance, i) for i in devices if i - distance in devices]
    return lax.ppermute(block, axis, route)


def intersection_weights(span_start, span_end, span_lengths, first_position, position_count):
    byte_first = (first_position + jnp.arange(position_count, dtype=jnp.int32)) * STRIDE
    lower_edge = jnp.maximum(span_start[:, None], byte_first[None, :])
    upper_edge = jnp.minimum(span_end[:, None], byte_first[None, :] + STRIDE)
    covered = jnp.maximum(upper_edge - lower_edge, 0).astype(jnp.float32)
    return (covered / span_lengths[:, None].astype(jnp.float32)).astype(jnp.bfloat16)


def local(byte_acts, conv_weight, conv_bias, proj_weight, teacher, span_lengths):
    byte_rows = byte_acts[0]
    row_total, width = byte_rows.shape
    groups_here = conv_weight.shape[0]
    group_width = width // groups_here
    positions = row_total // STRIDE
    seq_count = lax.axis_size("seq")
    seq_rank = lax.axis_index("seq")
    lengths_doc = span_lengths[0]
    tokens_all = lengths_doc.shape[0]
    span_end = jnp.cumsum(lengths_doc)
    span_start = span_end - lengths_doc
    next_rows = shifted(byte_rows[:STRIDE], "seq", -1)
    extended = jnp.concatenate([byte_rows, next_rows], axis=0)
    blocks = extended.reshape(positions + 1, STRIDE, groups_here, group_width)
    windows = jnp.concatenate([blocks[:-1], blocks[1:]], axis=1)
    taps_weight = conv_weight.reshape(groups_here, KERNEL, group_width, group_width)
    conv_out = jnp.einsum(
        "pkgc,gkco->pgo", windows, taps_weight, preferred_element_type=jnp.float32
    )
    conv_out = conv_out + conv_bias.reshape(groups_here, group_width)[None]
    downsampled = conv_out.reshape(positions, width).astype(jnp.bfloat16)
    local_weight = intersection_weights(
        span_start, span_end, lengths_doc, seq_rank * positions, positions
    )
    weight_part = local_weight
    pooled_sum = lax.psum_scatter(
        jnp.dot(weight_part, downsampled, preferred_element_type=jnp.float32).astype(jnp.bfloat16),
        "seq",
        scatter_dimension=0,
        tiled=True,
    )
    gathered = lax.all_gather(pooled_sum, "tensor", axis=1, tiled=True)
    predicted = jnp.dot(gathered, proj_weight, preferred_element_type=jnp.float32)
    err_grad = (predicted - teacher[0].astype(jnp.float32)).astype(jnp.bfloat16)
    proj_local = lax.dot_general(
        gathered, err_grad, (((0,), (0,)), ((), ())), preferred_element_type=jnp.float32
    )
    token_scale = 1.0 / jnp.sqrt(jnp.float32(lax.axis_size("dp") * tokens_all))
    proj_summed = lax.psum(proj_local.astype(jnp.bfloat16), ("dp", "seq")).astype(jnp.float32)
    proj_grad = proj_summed * token_scale
    weight_part = proj_weight
    pooled_grad_t = lax.psum_scatter(
        lax.dot_general(
            weight_part, err_grad, (((1,), (1,)), ((), ())), preferred_element_type=jnp.float32
        ).astype(jnp.bfloat16),
        "tensor",
        scatter_dimension=0,
        tiled=True,
    )
    weight_part = local_weight
    down_sum = lax.dot_general(
        weight_part,
        lax.all_gather(pooled_grad_t, "seq", axis=1, tiled=True),
        (((0,), (1,)), ((), ())),
        preferred_element_type=jnp.float32,
    )
    down_grad = down_sum.astype(jnp.bfloat16).reshape(positions, groups_here, group_width)
    conv_local = jnp.einsum(
        "pkgc,pgo->gkco", windows, down_grad, preferred_element_type=jnp.float32
    )
    conv_summed = lax.psum(conv_local.astype(jnp.bfloat16), ("dp", "seq")).astype(jnp.float32)
    position_scale = 1.0 / jnp.sqrt(jnp.float32(lax.axis_size("dp") * positions * seq_count))
    conv_grad = (conv_summed * position_scale).reshape(
        groups_here, KERNEL * group_width, group_width
    )
    window_grad = jnp.einsum(
        "pgo,gkco->pkgc", down_grad, taps_weight, preferred_element_type=jnp.float32
    )
    incoming = shifted(window_grad[-1, STRIDE:], "seq", 1)
    carried_grad = jnp.concatenate([incoming[None], window_grad[:-1, STRIDE:]], axis=0)
    byte_grad = (
        (window_grad[:, :STRIDE] + carried_grad).reshape(row_total, width).astype(jnp.bfloat16)
    )
    return (downsampled[None], byte_grad[None], conv_grad, proj_grad)


def solution(mesh):
    return jax.shard_map(
        local,
        mesh=mesh,
        in_specs=(
            P("dp", "seq", "tensor"),
            P("tensor", None, None),
            P("tensor"),
            P(None, "tensor"),
            P("dp", "seq", "tensor"),
            P("dp", None),
        ),
        out_specs=(
            P("dp", "seq", "tensor"),
            P("dp", "seq", "tensor"),
            P("tensor", None, None),
            P(None, "tensor"),
        ),
        check_vma=False,
    )
```

profile of v0, /device:TPU:1, one launch (start us, length us, event | category | flops | bytes accessed | tf_op | source)
XLA Modules:
  0.0 448.6 jit_solution(9548664783384587583)
XLA Ops:
  7.2 0.8 slice_bitcast_fusion
  8.1 5.1 %collective-permute-start = (bf16[4,128]{1,0:T(4,128)(2,1)S(1)}, bf16[4,128]{1,0:T(4,128)(2,1)S(1)}, u32[]{:S(2)}, u32[]{:S(2)}) collective-permute-start(bf16[4,128]{1,0:T(4,128)(2,1)S(1)} %slice_bitcast_fusion), channel_id=1, source_target_pairs={{16,0},{32,16},{48,32},{17,1},{33,17},{49,33},{18,2},{34,18},{50,3... | collective-permute-start | bytes 3080 | tf_op jit(solution)/shard_map/ppermute | solution.py:13
  13.2 1.0 reduce-window.9
  14.5 0.8 fusion.23
  15.3 0.7 convert_element_type.87
  16.0 1.4 copy.17
  17.4 1.5 pad_maximum_fusion
  19.1 1.0 copy-done.1
  20.0 0.7 fusion.11
  20.8 0.7 copy-done.7
  21.5 7.5 %fusion.2 = bf16[4096,128]{1,0:T(8,128)(2,1)} fusion(f32[4096]{0:T(1024)S(1)} %convert_element_type.87, s32[1024]{0:T(1024)S(1)} %add_multiply_fusion, s32[4096]{0:T(1024)S(1)} %get-tuple-element.6, s32[1024]{0:T(1024)S(1)} %broadcast_add_fusion, s32[4096]{0:T(1024)S(1)} %get-tuple-element.7, bf16[1,128,1024]{1,2,0:T(8,128)(2,1)S(1)} %fusion.11), kind=kOutput, calls=%fused_computation.3 | convolution fusion | flops 1103626240 | bytes 1368064 | tf_op jit(solution)/shard_map/dot_general | solution.py:51
  29.0 38.1 %reduce-scatter.5.cloned.1.call-done = bf16[1024,128]{1,0:T(8,128)(2,1)} async-done(((bf16[4096,128]{1,0:T(8,128)(2,1)}), bf16[1024,128]{1,0:T(8,128)(2,1)}) %reduce-scatter.5.cloned.1.call-update) | async-done | bytes 262160 | tf_op jit(solution)/shard_map/reduce_scatter | solution.py:50
  67.2 80.8 %all-gather.3.cloned.1.call-done = bf16[1024,2048]{1,0:T(8,128)(2,1)} async-done(((bf16[1024,128]{1,0:T(8,128)(2,1)}), bf16[1024,2048]{1,0:T(8,128)(2,1)}) %all-gather.3.cloned.1.call-update) | async-done | bytes 4194320 | tf_op jit(solution)/shard_map/all_gather | solution.py:56
  148.1 4.6 %fusion.24 = f32[1024,512]{1,0:T(8,128)S(1)} fusion(bf16[1024,2048]{1,0:T(8,128)(2,1)} %all-gather.3.cloned.1.call-done, bf16[2048,512]{1,0:T(8,128)(2,1)S(1)} %copy-done), kind=kOutput, calls=%fused_computation.37 | convolution fusion | flops 2147483648 | bytes 8388608 | tf_op jit(solution)/shard_map/dot_general | solution.py:57
  152.7 1.4 copy-done.8
  154.0 4.4 convert_bitcast_fusion
  158.4 6.4 %copy.23 = bf16[2048,1024]{1,0:T(8,128)(2,1)} copy(bf16[2048,1024]{0,1:T(8,128)(2,1)} %convert_bitcast_fusion) | data formatting | bytes 8388608
  164.9 78.6 %reduce-scatter.7.cloned.1.call-done = bf16[128,1024]{1,0:T(8,128)(2,1)} async-done(((bf16[2048,1024]{1,0:T(8,128)(2,1)}), bf16[128,1024]{1,0:T(8,128)(2,1)}) %reduce-scatter.7.cloned.1.call-update) | async-done | bytes 262160
  243.5 1.8 copy.24
  245.6 6.8 %convolution_convert_fusion = bf16[2048,512]{1,0:T(8,128)(2,1)} fusion(bf16[1024,2048]{1,0:T(8,128)(2,1)} %all-gather.3.cloned.1.call-done, f32[1024,512]{1,0:T(8,128)} %copy-done.8, bf16[1,1024,512]{2,1,0:T(8,128)(2,1)} %param.10), kind=kOutput, calls=%fused_computation.6 | convolution fusion | flops 2150105088 | bytes 9437184 | tf_op jit(solution)/shard_map/dot_general | solution.py:59
  252.3 24.2 %all-gather.5.cloned.1.call-done = bf16[128,4096]{0,1:T(8,128)(2,1)} async-done(((bf16[128,1024]{0,1:T(8,128)(2,1)}), bf16[128,4096]{0,1:T(8,128)(2,1)}) %all-gather.5.cloned.1.call-update) | async-done | bytes 1048592 | tf_op jit(solution)/shard_map/all_gather | solution.py:77
  276.5 7.7 %fusion.15 = bf16[1024,128,1]{1,0,2:T(8,128)(2,1)S(1)} fusion(bf16[128,4096]{0,1:T(8,128)(2,1)} %all-gather.5.cloned.1.call-done, f32[4096]{0:T(1024)S(1)} %convert_element_type.87, s32[1024]{0:T(1024)S(1)} %add_multiply_fusion, s32[4096]{0:T(1024)S(1)} %get-tuple-element.6, s32[1024]{0:T(1024)S(1)} %broadcast_add_fusion, s32[4096]{0:T(1024)S(1)} %get-tuple-element.7), kind=kOutput, calls=%fused_computation.21 | convolution fusion | flops 1103233024 | bytes 1368064 | tf_op jit(solution)/shard_map/dot_general | solution.py:75
  284.2 0.7 copy-done.4
  284.9 1.4 fusion.14
  286.4 1.7 convolution_bitcast_fusion
  288.1 2.1 collective-permute-start.1
  290.3 0.8 collective-permute-done.1
  291.1 0.3 fusion.3
  291.4 1.8 copy.20
  293.2 142.9 %all-reduce.3.cloned.1.call-done = (bf16[1,8,128,128]{3,2,1,0:T(8,128)(2,1)}, bf16[2048,512]{1,0:T(8,128)(2,1)}) async-done(((bf16[1,8,128,128]{3,2,1,0:T(8,128)(2,1)}, bf16[2048,512]{1,0:T(8,128)(2,1)}), (bf16[1,8,128,128]{3,2,1,0:T(8,128)(2,1)}, bf16[2048,512]{1,0:T(8,128)(2,1)})) %all-reduce.3.cloned.1.call-update) | async-done | bytes 2359312 | tf_op jit(solution)/shard_map/psum | solution.py:85
  436.1 1.8 convert_multiply_fusion.1
  437.9 4.2 convert_multiply_fusion
  (33 shorter events, 1.0 us)
Async XLA Ops:
  7.2 140.9 %copy-start = (bf16[2048,512]{1,0:T(8,128)(2,1)S(1)}, bf16[2048,512]{1,0:T(8,128)(2,1)}, u32[]{:S(2)}) copy-start(bf16[2048,512]{1,0:T(8,128)(2,1)} %param.9) | copy-start | bytes 6291460
  7.2 12.8 %copy-start.6 = (f32[128]{0:T(128)S(1)}, f32[128]{0:T(128)}, u32[]{:S(2)}) copy-start(f32[128]{0:T(128)} %param.8) | copy-start | bytes 1540
  7.2 12.8 %copy-start.3 = (bf16[1,1024,128]{2,1,0:T(8,128)(2,1)S(1)}, bf16[1,1024,128]{2,1,0:T(8,128)(2,1)}, u32[]{:S(2)}) copy-start(bf16[1,1024,128]{2,1,0:T(8,128)(2,1)} %param.7) | copy-start | bytes 786436
  7.2 60.0 %reduce-scatter.5.cloned.1.call-start = ((), (), s32[]{:S(2)}) async-start(), calls=%async_computation.2 | async-start | bytes 1310720 | tf_op jit(solution)/shard_map/reduce_scatter | solution.py:50
  8.1 9.3 %collective-permute-start = (bf16[4,128]{1,0:T(4,128)(2,1)S(1)}, bf16[4,128]{1,0:T(4,128)(2,1)S(1)}, u32[]{:S(2)}, u32[]{:S(2)}) collective-permute-start(bf16[4,128]{1,0:T(4,128)(2,1)S(1)} %slice_bitcast_fusion), channel_id=1, source_target_pairs={{16,0},{32,16},{48,32},{17,1},{33,17},{49,33},{18,2},{34,18},{50,3... | collective-permute-start | bytes 3080 | tf_op jit(solution)/shard_map/ppermute | solution.py:13
  19.0 1.0 copy-start.1
  20.7 0.7 copy-start.7
  29.0 119.1 %all-gather.3.cloned.1.call-start = ((), (), s32[]{:S(2)}) async-start(), calls=%async_computation.3 | async-start | bytes 4456448 | tf_op jit(solution)/shard_map/all_gather | solution.py:56
  67.2 176.3 %reduce-scatter.7.cloned.1.call-start = ((), (), s32[]{:S(2)}) async-start(), calls=%async_computation.5 | async-start | bytes 4456448
  148.1 6.0 %copy-start.5 = (bf16[1,1024,512]{2,1,0:T(8,128)(2,1)S(1)}, bf16[1,1024,512]{2,1,0:T(8,128)(2,1)}, u32[]{:S(2)}) copy-start(bf16[1,1024,512]{2,1,0:T(8,128)(2,1)} %param.10) | copy-start | bytes 3145732
  152.7 1.4 copy-start.8
  164.9 111.6 %all-gather.5.cloned.1.call-start = ((), (), s32[]{:S(2)}) async-start(), calls=%async_computation.4 | async-start | bytes 1310720 | tf_op jit(solution)/shard_map/all_gather | solution.py:77
  245.3 190.8 %all-reduce.3.cloned.1.call-start = ((), (), s32[]{:S(2)}) async-start(), calls=%async_computation.6 | async-start | bytes 4718592 | tf_op jit(solution)/shard_map/psum | solution.py:85
  276.5 8.4 %copy-start.2 = (bf16[1024,4,1,128]{3,0,1,2:T(8,128)(2,1)S(1)}, bf16[1024,4,1,128]{3,0,1,2:T(8,128)(2,1)}, u32[]{:S(2)}) copy-start(bf16[1024,4,1,128]{3,0,1,2:T(8,128)(2,1)} %copy-done.1) | copy-start | bytes 3145732
  284.2 0.7 copy-start.4
  288.1 3.1 collective-permute-start.1
Sparse Core Ops, SparseCore 0:
  29.1 38.0 reduce-scatter.4
  69.0 79.0 all-gather.2
  165.0 78.4 reduce-scatter.6
  245.9 30.5 all-gather.4
  286.5 149.5 all-reduce.2
where the time goes:
time: 449 us
  waiting for transfers between devices  366 us (82%)
  matrix products  34.8 us (8%)
  local copies, waits for them, and re-layouts  16.4 us (4%)
  between operations  13.9 us (3%)
  other arithmetic  10.3 us (2%)
  starting transfers between devices  7.58 us (2%)
    psum x1, waiting for transfers between devices, local(): lax.psum(conv_local.astype(jnp.bfloat16), ('dp', 'seq')).astype(jnp.float32)  143 us
    all_gather x1, waiting for transfers between devices, local(): gathered = lax.all_gather(pooled_sum, 'tensor', axis=1, tiled=True)  80.8 us
    unnamed x6, waiting for transfers between devices  78.7 us
    reduce_scatter x1, waiting for transfers between devices, local(): lax.psum_scatter(jnp.dot(weight_part, downsampled, preferred_element_type...  38.1 us
    all_gather x1, waiting for transfers between devices, local(): lax.all_gather(pooled_grad_t, 'seq', axis=1, tiled=True)  24.2 us
    unnamed x20, local copies, waits for them, and re-layouts  12 us
  transfers between devices with their start and end apart: 7, of which 6 were waited for; matrix products, arithmetic and copies ran while one was open for 3% of the time, Pallas kernels for 0%

commit v1 on v0

--- a/solution.py
+++ b/solution.py
@@ -82,7 +82,9 @@
     conv_local = jnp.einsum(
         "pkgc,pgo->gkco", windows, down_grad, preferred_element_type=jnp.float32
     )
-    conv_summed = lax.psum(conv_local.astype(jnp.bfloat16), ("dp", "seq")).astype(jnp.float32)
+    conv_summed = jnp.sum(
+        lax.all_gather(conv_local.astype(jnp.bfloat16), ("dp", "seq")), axis=0
+    ).astype(jnp.float32)
     position_scale = 1.0 / jnp.sqrt(jnp.float32(lax.axis_size("dp") * positions * seq_count))
     conv_grad = (conv_summed * position_scale).reshape(
         groups_here, KERNEL * group_width, group_width

time: 449 us -> 505 us (1.12)
  waiting for transfers between devices: 366 us -> 417 us
    all_gather x0 -> x1, waiting for transfers between devices: none -> 59.2 us  [local(): lax.all_gather(conv_local.astype(jnp.bfloat16), ('dp', 'seq'))]
    psum x1, waiting for transfers between devices: 143 us -> 136 us  [local(): lax.psum(proj_local.astype(jnp.bfloat16), ('dp', 'seq')).astype(jnp.float32)]
    unnamed x20 -> x24, local copies, waits for them, and re-layouts: 12 us -> 13.9 us
    unnamed x6 -> x7, waiting for transfers between devices: 78.7 us -> 78.7 us
  transfers between devices with their start and end apart: 7 -> 8, of which waited for: 6 -> 6; matrix products, arithmetic and copies ran while one was open for 3% -> 6% of each run, Pallas kernels for 0% -> 0%
where the time goes in v1:
time: 505 us; the launch traced here: 504 us
  waiting for transfers between devices  417 us (83%)
  matrix products  34.8 us (7%)
  local copies, waits for them, and re-layouts  18.4 us (4%)
  between operations  14.3 us (3%)
  other arithmetic  12.5 us (2%)
  starting transfers between devices  7.61 us (2%)
    psum x1, waiting for transfers between devices, local(): lax.psum(proj_local.astype(jnp.bfloat16), ('dp', 'seq')).astype(jnp.float32)  136 us
    all_gather x1, waiting for transfers between devices, local(): gathered = lax.all_gather(pooled_sum, 'tensor', axis=1, tiled=True)  80.8 us
    unnamed x7, waiting for transfers between devices  78.7 us
    all_gather x1, waiting for transfers between devices, local(): lax.all_gather(conv_local.astype(jnp.bfloat16), ('dp', 'seq'))  59.2 us
    reduce_scatter x1, waiting for transfers between devices, local(): lax.psum_scatter(jnp.dot(weight_part, downsampled, preferred_element_type...  38.1 us
    all_gather x1, waiting for transfers between devices, local(): lax.all_gather(pooled_grad_t, 'seq', axis=1, tiled=True)  24.1 us
    unnamed x24, local copies, waits for them, and re-layouts  13.9 us
  transfers between devices with their start and end apart: 8, of which 6 were waited for; matrix products, arithmetic and copies ran while one was open for 6% of the time, Pallas kernels for 0%

profile of v1, /device:TPU:1, one launch (start us, length us, event | category | flops | bytes accessed | tf_op | source)
XLA Modules:
  0.0 504.5 jit_solution(6166291398364459517)
XLA Ops:
  7.2 0.8 slice_bitcast_fusion
  8.1 5.1 %collective-permute-start = (bf16[4,128]{1,0:T(4,128)(2,1)S(1)}, bf16[4,128]{1,0:T(4,128)(2,1)S(1)}, u32[]{:S(2)}, u32[]{:S(2)}) collective-permute-start(bf16[4,128]{1,0:T(4,128)(2,1)S(1)} %slice_bitcast_fusion), channel_id=1, source_target_pairs={{16,0},{32,16},{48,32},{17,1},{33,17},{49,33},{18,2},{34,18},{50,3... | collective-permute-start | bytes 3080 | tf_op jit(solution)/shard_map/ppermute | solution.py:13
  13.2 1.0 reduce-window.9
  14.5 0.8 fusion.22
  15.3 0.7 convert_element_type.97
  16.0 1.4 copy.17
  17.4 1.5 pad_maximum_fusion
  19.1 1.0 copy-done.3
  20.0 0.7 fusion.11
  20.8 0.7 copy-done.9
  21.5 7.5 %fusion.2 = bf16[4096,128]{1,0:T(8,128)(2,1)} fusion(f32[4096]{0:T(1024)S(1)} %convert_element_type.97, s32[1024]{0:T(1024)S(1)} %add_multiply_fusion, s32[4096]{0:T(1024)S(1)} %get-tuple-element.4, s32[1024]{0:T(1024)S(1)} %broadcast_add_fusion, s32[4096]{0:T(1024)S(1)} %get-tuple-element.5, bf16[1,128,1024]{1,2,0:T(8,128)(2,1)S(1)} %fusion.11), kind=kOutput, calls=%fused_computation.3 | convolution fusion | flops 1103626240 | bytes 1368064 | tf_op jit(solution)/shard_map/dot_general | solution.py:51
  29.0 38.1 %reduce-scatter.5.cloned.1.call-done = bf16[1024,128]{1,0:T(8,128)(2,1)} async-done(((bf16[4096,128]{1,0:T(8,128)(2,1)}), bf16[1024,128]{1,0:T(8,128)(2,1)}) %reduce-scatter.5.cloned.1.call-update) | async-done | bytes 262160 | tf_op jit(solution)/shard_map/reduce_scatter | solution.py:50
  67.2 80.8 %all-gather.5.cloned.1.call-done = bf16[1024,2048]{1,0:T(8,128)(2,1)} async-done(((bf16[1024,128]{1,0:T(8,128)(2,1)}), bf16[1024,2048]{1,0:T(8,128)(2,1)}) %all-gather.5.cloned.1.call-update) | async-done | bytes 4194320 | tf_op jit(solution)/shard_map/all_gather | solution.py:56
  148.1 4.6 fusion.23
  152.7 1.4 copy-done.10
  154.0 4.4 convert_bitcast_fusion
  158.4 6.4 %copy.23 = bf16[2048,1024]{1,0:T(8,128)(2,1)} copy(bf16[2048,1024]{0,1:T(8,128)(2,1)} %convert_bitcast_fusion) | data formatting | bytes 8388608
  164.9 78.6 %reduce-scatter.7.cloned.1.call-done = bf16[128,1024]{1,0:T(8,128)(2,1)} async-done(((bf16[2048,1024]{1,0:T(8,128)(2,1)}), bf16[128,1024]{1,0:T(8,128)(2,1)}) %reduce-scatter.7.cloned.1.call-update) | async-done | bytes 262160
  243.5 1.8 copy.24
  245.4 6.8 %convolution_convert_fusion = bf16[2048,512]{1,0:T(8,128)(2,1)} fusion(bf16[1024,2048]{1,0:T(8,128)(2,1)} %all-gather.5.cloned.1.call-done, f32[1024,512]{1,0:T(8,128)} %copy-done.10, bf16[1,1024,512]{2,1,0:T(8,128)(2,1)} %param.10), kind=kOutput, calls=%fused_computation.6 | convolution fusion | flops 2150105088 | bytes 9437184 | tf_op jit(solution)/shard_map/dot_general | solution.py:59
  252.4 24.1 %all-gather.7.cloned.1.call-done = bf16[128,4096]{0,1:T(8,128)(2,1)} async-done(((bf16[128,1024]{0,1:T(8,128)(2,1)}), bf16[128,4096]{0,1:T(8,128)(2,1)}) %all-gather.7.cloned.1.call-update) | async-done | bytes 1048592 | tf_op jit(solution)/shard_map/all_gather | solution.py:77
  276.5 7.7 %fusion.14 = bf16[1024,128,1]{1,0,2:T(8,128)(2,1)S(1)} fusion(bf16[128,4096]{0,1:T(8,128)(2,1)} %all-gather.7.cloned.1.call-done, f32[4096]{0:T(1024)S(1)} %convert_element_type.97, s32[1024]{0:T(1024)S(1)} %add_multiply_fusion, s32[4096]{0:T(1024)S(1)} %get-tuple-element.4, s32[1024]{0:T(1024)S(1)} %broadcast_add_fusion, s32[4096]{0:T(1024)S(1)} %get-tuple-element.5), kind=kOutput, calls=%fused_computation.20 | convolution fusion | flops 1103233024 | bytes 1368064 | tf_op jit(solution)/shard_map/dot_general | solution.py:75
  284.9 1.5 fusion.12
  286.4 1.7 convolution_bitcast_fusion
  288.1 2.0 copy-done.1
  290.0 2.1 collective-permute-start.1
  292.1 135.9 %all-reduce.2.cloned.1.call-done = bf16[2048,512]{1,0:T(8,128)(2,1)} async-done(((bf16[2048,512]{1,0:T(8,128)(2,1)}), bf16[2048,512]{1,0:T(8,128)(2,1)}) %all-reduce.2.cloned.1.call-update) | async-done | bytes 2097168 | tf_op jit(solution)/shard_map/psum | solution.py:63
  428.0 4.3 convert_multiply_fusion
  432.8 1.8 copy.20
  434.6 59.2 %all-gather.9.cloned.1.call-done = bf16[128,128,128]{2,1,0:T(8,128)(2,1)} async-done(((bf16[8,128,128]{2,1,0:T(8,128)(2,1)}), bf16[128,128,128]{2,1,0:T(8,128)(2,1)}) %all-gather.9.cloned.1.call-update) | async-done | bytes 4194320 | tf_op jit(solution)/shard_map/all_gather | solution.py:86
  493.8 3.0 reduce.2
  496.8 0.8 convert_multiply_fusion.1
  (41 shorter events, 2.1 us)
Async XLA Ops:
  7.2 140.9 %copy-start = (bf16[2048,512]{1,0:T(8,128)(2,1)S(1)}, bf16[2048,512]{1,0:T(8,128)(2,1)}, u32[]{:S(2)}) copy-start(bf16[2048,512]{1,0:T(8,128)(2,1)} %param.9) | copy-start | bytes 6291460
  7.2 12.8 %copy-start.8 = (f32[128]{0:T(128)S(1)}, f32[128]{0:T(128)}, u32[]{:S(2)}) copy-start(f32[128]{0:T(128)} %param.8) | copy-start | bytes 1540
  7.2 12.8 %copy-start.5 = (bf16[1,1024,128]{2,1,0:T(8,128)(2,1)S(1)}, bf16[1,1024,128]{2,1,0:T(8,128)(2,1)}, u32[]{:S(2)}) copy-start(bf16[1,1024,128]{2,1,0:T(8,128)(2,1)} %param.7) | copy-start | bytes 786436
  7.2 60.0 %reduce-scatter.5.cloned.1.call-start = ((), (), s32[]{:S(2)}) async-start(), calls=%async_computation.2 | async-start | bytes 1310720 | tf_op jit(solution)/shard_map/reduce_scatter | solution.py:50
  8.1 9.3 %collective-permute-start = (bf16[4,128]{1,0:T(4,128)(2,1)S(1)}, bf16[4,128]{1,0:T(4,128)(2,1)S(1)}, u32[]{:S(2)}, u32[]{:S(2)}) collective-permute-start(bf16[4,128]{1,0:T(4,128)(2,1)S(1)} %slice_bitcast_fusion), channel_id=1, source_target_pairs={{16,0},{32,16},{48,32},{17,1},{33,17},{49,33},{18,2},{34,18},{50,3... | collective-permute-start | bytes 3080 | tf_op jit(solution)/shard_map/ppermute | solution.py:13
  19.0 1.0 copy-start.3
  20.7 0.7 copy-start.9
  29.0 119.1 %all-gather.5.cloned.1.call-start = ((), (), s32[]{:S(2)}) async-start(), calls=%async_computation.3 | async-start | bytes 4456448 | tf_op jit(solution)/shard_map/all_gather | solution.py:56
  67.2 176.3 %reduce-scatter.7.cloned.1.call-start = ((), (), s32[]{:S(2)}) async-start(), calls=%async_computation.7 | async-start | bytes 4456448
  148.1 6.0 %copy-start.7 = (bf16[1,1024,512]{2,1,0:T(8,128)(2,1)S(1)}, bf16[1,1024,512]{2,1,0:T(8,128)(2,1)}, u32[]{:S(2)}) copy-start(bf16[1,1024,512]{2,1,0:T(8,128)(2,1)} %param.10) | copy-start | bytes 3145732
  152.7 1.4 copy-start.10
  164.9 111.6 %all-gather.7.cloned.1.call-start = ((), (), s32[]{:S(2)}) async-start(), calls=%async_computation.4 | async-start | bytes 1310720 | tf_op jit(solution)/shard_map/all_gather | solution.py:77
  245.3 182.7 %all-reduce.2.cloned.1.call-start = ((), (), s32[]{:S(2)}) async-start(), calls=%async_computation.5 | async-start | bytes 4194304 | tf_op jit(solution)/shard_map/psum | solution.py:63
  252.2 241.6 %all-gather.9.cloned.1.call-start = ((), (), s32[]{:S(2)}) async-start(), calls=%async_computation.6 | async-start | bytes 4456448 | tf_op jit(solution)/shard_map/all_gather | solution.py:86
  276.5 8.4 %copy-start.4 = (bf16[1024,4,1,128]{3,0,1,2:T(8,128)(2,1)S(1)}, bf16[1024,4,1,128]{3,0,1,2:T(8,128)(2,1)}, u32[]{:S(2)}) copy-start(bf16[1024,4,1,128]{3,0,1,2:T(8,128)(2,1)} %copy-done.3) | copy-start | bytes 3145732
  284.2 0.7 copy-start.6
  288.1 2.0 copy-start.1
  290.0 142.5 %collective-permute-start.1 = (f32[4,1,128]{2,0,1:T(4,128)S(1)}, f32[4,1,128]{2,0,1:T(4,128)S(1)}, u32[]{:S(2)}, u32[]{:S(2)}) collective-permute-start(f32[4,1,128]{2,0,1:T(4,128)S(1)} %bitcast.89), channel_id=1, source_target_pairs={{0,16},{16,32},{32,48},{1,17},{17,33},{33,49},{2,18},{18,34},{34,5... | collective-permute-start | bytes 6152 | tf_op jit(solution)/shard_map/ppermute | solution.py:13
  428.0 4.4 copy-start.2
Sparse Core Ops, SparseCore 0:
  29.1 38.0 reduce-scatter.4
  69.0 79.0 all-gather.4
  165.0 78.4 reduce-scatter.6
  245.9 30.5 all-gather.6
  279.8 148.2 all-reduce.1
  430.9 62.8 all-gather.8
